TPU v7x, 512 devices: a whole 4x8x8 slice. The times are simulated.
512 devices in a mesh: ctx: 64 (over z_lo, y, core), ch: 8 (over z_hi, x).
Axes of the slice: x: 4, y: 8, z: 8 (z_hi: 2, z_lo: 4; z = z_hi * 4 + z_lo), core: 2. Of those that a mesh axis runs over, the one named last changes fastest.
Arguments:
- query_in: bfloat16 [16384, 4096], P('ctx', 'ch'), may hold values from -6 to 6
- key_in: bfloat16 [16384, 4096], P('ctx', 'ch'), may hold values from -6 to 6
- value_in: bfloat16 [16384, 4096], P('ctx', 'ch'), may hold values from -6 to 6
- short_weight: float32 [3, 3, 4096], P(None, None, 'ch'), may hold values from -3 to 3
- long_filter: bfloat16 [32, 768], P('ch'), may hold values from -1.1 to 1.1
- skip_weight: float32 [4096], P('ch'), may hold values from -1 to 1
- out_weight: bfloat16 [4096, 4096], P('ctx', 'ch'), may hold values from -0.09375 to 0.09375
- doc_ids: int32 [16384], P('ctx'), may hold values from 0 to 41, as said below
- out_grad: bfloat16 [16384, 4096], P('ctx', 'ch'), may hold values from -6 to 6
Outputs:
- layer_out: bfloat16 [16384, 4096], P('ctx', 'ch')
- grad_query: bfloat16 [16384, 4096], P('ctx', 'ch')
- grad_key: bfloat16 [16384, 4096], P('ctx', 'ch')
- grad_value: bfloat16 [16384, 4096], P('ctx', 'ch')
Inputs may be any that keep to these rules, and one draw needn't show every extreme that they name: doc_ids never falls along the tokens; every number from 0 to 41 occurs; every document has at most 768 tokens and one has exactly 768.
All inputs are finite; a program needn't handle non-finite values.
Results may differ from a plain program's by a relative error of at most 0.0058.
Values may be sent and summed in bfloat16 or wider, within the bound.
No kernel may reach another device: no remote copies, remote signals or barrier semaphores. Data moves between devices by JAX's collectives and lax.ppermute only.
A program may use at most 64 MiB of HBM per device.

v0:
```python
import jax
import jax.numpy as jnp
from jax import lax
from jax.sharding import PartitionSpec as P

HOPS = 3


def shifted(array, axis, by):
    size = lax.axis_size(axis)
    pairs = [(i, i + by) for i in range(size) if 0 <= i + by < size]
    return lax.ppermute(array, axis, pairs)


def toeplitz_tiles(long_filter, row_count, hop_count):
    group_count, span_len = long_filter.shape
    padded = jnp.concatenate(
        [
            jnp.zeros((group_count, row_count), long_filter.dtype),
            long_filter,
            jnp.zeros((group_count, (hop_count + 3) * row_count - span_len), long_filter.dtype),
        ],
        axis=1,
    )
    tiles_list = []
    for distance in range(hop_count + 1):
        window = padded[:, distance * row_count + 1 : distance * row_count + 1 + 2 * row_count]
        cyclic = jnp.concatenate(
            [
                window[:, row_count - 1 : 2 * row_count - 1],
                jnp.zeros((group_count, 1), window.dtype),
                window[:, : row_count - 1],
            ],
            axis=1,
        )
        repeated = jnp.tile(cyclic, (1, row_count))[:, : row_count * (2 * row_count - 1)]
        tiles_list.append(
            repeated.reshape(group_count, row_count, 2 * row_count - 1)[:, :, :row_count]
        )
    return tiles_list


def apply_forward(band_tile, source):
    row_count, channels = source.shape
    grouped = source.reshape(row_count, band_tile.shape[0], -1)
    return jnp.einsum(
        "gst,sgc->tgc", band_tile, grouped, preferred_element_type=jnp.float32
    ).reshape(row_count, channels)


def apply_adjoint(band_tile, source):
    row_count, channels = source.shape
    grouped = source.reshape(row_count, band_tile.shape[0], -1)
    return jnp.einsum(
        "gst,tgc->sgc", band_tile, grouped, preferred_element_type=jnp.float32
    ).reshape(row_count, channels)


def causal_taps(extended, weights, ext_ids, doc_ids):
    row_count = doc_ids.shape[0]
    summed = jnp.zeros((row_count, extended.shape[1]), jnp.float32)
    for offset in range(3):
        first_row = 2 - offset
        same_doc = ext_ids[first_row : first_row + row_count] == doc_ids
        summed = summed + jnp.where(
            same_doc[:, None],
            weights[offset][None, :]
            * extended[first_row : first_row + row_count].astype(jnp.float32),
            0.0,
        )
    return summed


def anti_taps(extended, weights, ext_ids, doc_ids):
    row_count = doc_ids.shape[0]
    summed = jnp.zeros((row_count, extended.shape[1]), jnp.float32)
    for offset in range(3):
        same_doc = ext_ids[offset : offset + row_count] == doc_ids
        summed = summed + jnp.where(
            same_doc[:, None],
            weights[offset][None, :] * extended[offset : offset + row_count].astype(jnp.float32),
            0.0,
        )
    return summed


def local(
    query_in,
    key_in,
    value_in,
    short_weight,
    long_filter,
    skip_weight,
    out_weight,
    doc_ids,
    out_grad,
):
    row_count, channels = query_in.shape
    before_ids = shifted(doc_ids[-2:] + 1, "ctx", 1) - 1
    after_ids = shifted(doc_ids[:2] + 1, "ctx", -1) - 1
    first_id = doc_ids[0]
    last_id = doc_ids[-1]
    prev_last = before_ids[1]
    next_first = after_ids[0]
    single_doc = first_id == last_id
    joins_next = next_first == last_id
    joins_prev = prev_last == first_id
    prev_rows = shifted((query_in[-2:], key_in[-2:], value_in[-2:]), "ctx", 1)
    back_ids = jnp.concatenate([before_ids, doc_ids])
    query_short = causal_taps(
        jnp.concatenate([prev_rows[0], query_in]), short_weight[0], back_ids, doc_ids
    )
    key_short = causal_taps(
        jnp.concatenate([prev_rows[1], key_in]), short_weight[1], back_ids, doc_ids
    )
    value_short = causal_taps(
        jnp.concatenate([prev_rows[2], value_in]), short_weight[2], back_ids, doc_ids
    )
    gated = (key_short * value_short).astype(jnp.bfloat16)
    tiles_list = toeplitz_tiles(long_filter, row_count, HOPS)
    same_doc = doc_ids[:, None] == doc_ids[None, :]
    diagonal = jnp.where(same_doc[None], tiles_list[0], jnp.zeros((), tiles_list[0].dtype))
    head_rows = (doc_ids == first_id)[:, None]
    tail_rows = (doc_ids == last_id)[:, None]
    zero_half = jnp.zeros((), gated.dtype)

    def cross_term(is_live, product, band_tile, source):
        summand = jnp.where(is_live, product(band_tile, source), 0.0)
        return summand

    mixed = apply_forward(diagonal, gated) + skip_weight[None, :] * gated.astype(jnp.float32)
    own_tail = jnp.where(tail_rows, gated, zero_half)
    moving = jnp.where(joins_next, own_tail, zero_half)
    for distance in range(1, HOPS + 1):
        moving = shifted(moving, "ctx", 1)
        is_live = jnp.any(moving != 0)
        mixed = mixed + jnp.where(
            head_rows, cross_term(is_live, apply_forward, tiles_list[distance], moving), 0.0
        )
        moving = jnp.where(single_doc & joins_next, moving, zero_half)
    pre_gate = (query_short * mixed).astype(jnp.bfloat16)
    weight_rows = lax.all_gather(out_weight, "ctx", axis=0, tiled=True)
    matched = weight_rows
    out_sum = jnp.dot(
        lax.all_gather(pre_gate, "ch", axis=1, tiled=True),
        matched,
        preferred_element_type=jnp.float32,
    )
    matched = weight_rows
    grad_cols = lax.psum_scatter(
        lax.dot_general(
            matched, out_grad, (((1,), (1,)), ((), ())), preferred_element_type=jnp.float32
        ),
        "ch",
        scatter_dimension=0,
        tiled=True,
    )
    layer_out = out_sum.astype(jnp.bfloat16)
    grad_pre = jnp.transpose(grad_cols)
    grad_query_short = (grad_pre * mixed).astype(jnp.bfloat16)
    grad_mixed = (grad_pre * query_short).astype(jnp.bfloat16)
    own_head = jnp.where(head_rows, grad_mixed, zero_half)
    grad_gated = apply_adjoint(diagonal, grad_mixed) + skip_weight[None, :] * grad_mixed.astype(
        jnp.float32
    )
    moving_back = jnp.where(joins_prev, own_head, zero_half)
    for distance in range(1, HOPS + 1):
        moving_back = shifted(moving_back, "ctx", -1)
        is_live = jnp.any(moving_back != 0)
        grad_gated = grad_gated + jnp.where(
            tail_rows, cross_term(is_live, apply_adjoint, tiles_list[distance], moving_back), 0.0
        )
        moving_back = jnp.where(single_doc & joins_prev, moving_back, zero_half)
    grad_key_short = (grad_gated * value_short).astype(jnp.bfloat16)
    grad_value_short = (grad_gated * key_short).astype(jnp.bfloat16)
    next_rows = shifted((grad_query_short[:2], grad_key_short[:2], grad_value_short[:2]), "ctx", -1)
    ahead_ids = jnp.concatenate([doc_ids, after_ids])
    grad_query = anti_taps(
        jnp.concatenate([grad_query_short, next_rows[0]]), short_weight[0], ahead_ids, doc_ids
    ).astype(jnp.bfloat16)
    grad_key = anti_taps(
        jnp.concatenate([grad_key_short, next_rows[1]]), short_weight[1], ahead_ids, doc_ids
    ).astype(jnp.bfloat16)
    grad_value = anti_taps(
        jnp.concatenate([grad_value_short, next_rows[2]]), short_weight[2], ahead_ids, doc_ids
    ).astype(jnp.bfloat16)
    return (layer_out, grad_query, grad_key, grad_value)


def solution(mesh):
    return jax.shard_map(
        local,
        mesh=mesh,
        in_specs=(
            P("ctx", "ch"),
            P("ctx", "ch"),
            P("ctx", "ch"),
            P(None, None, "ch"),
            P("ch", None),
            P("ch"),
            P("ctx", "ch"),
            P("ctx"),
            P("ctx", "ch"),
        ),
        out_specs=(P("ctx", "ch"), P("ctx", "ch"), P("ctx", "ch"), P("ctx", "ch")),
        check_vma=False,
    )
```

profile of v0, /device:TPU:8, one launch (start us, length us, event | category | flops | bytes accessed | tf_op | source)
XLA Modules:
  0.0 379.9 jit_solution(4327605552182288887)
XLA Ops:
  8.0 125.7 %all-gather.5.cloned.1.call-done = bf16[4096,512]{1,0:T(8,128)(2,1)} async-done(((bf16[64,512]{1,0:T(8,128)(2,1)}), bf16[4096,512]{1,0:T(8,128)(2,1)}) %all-gather.5.cloned.1.call-update) | async-done | bytes 4194320 | tf_op jit(solution)/shard_map/all_gather | solution.py:142
  133.6 5.5 %fusion.39 = f32[4096,256]{1,0:T(8,128)} fusion(bf16[4096,512]{1,0:T(8,128)(2,1)} %all-gather.5.cloned.1.call-done, bf16[256,512]{1,0:T(8,128)(2,1)S(1)} %copy-done), kind=kOutput, calls=%fused_computation.116 | convolution fusion | flops 1073741824 | bytes 8650752 | tf_op jit(solution)/shard_map/dot_general | solution.py:151
  140.4 3.6 collective-permute-start.4
  153.3 2.7 collective-permute-start.3
  165.0 3.3 select_select_fusion.1
  174.5 3.0 reshape.150
  179.7 3.1 reshape.148
  185.0 3.0 reshape.146
  191.4 4.0 %reshape.143 = bf16[4,256,511]{2,1,0:T(8,128)(2,1)} reshape(bf16[4,130816]{1,0:T(4,128)(2,1)} %slice.278) | data formatting | bytes 2093056 | tf_op jit(solution)/shard_map/reshape | solution.py:38
  198.6 3.6 collective-permute-start.6
  203.8 2.6 broadcast_select_fusion.5
  211.0 3.1 collective-permute-done.7
  216.6 59.5 %reduce-scatter.2.cloned.1.call-done = f32[512,256]{1,0:T(8,128)} async-done(((f32[4096,256]{1,0:T(8,128)}), f32[512,256]{1,0:T(8,128)}) %reduce-scatter.2.cloned.1.call-update) | async-done | bytes 524304 | tf_op jit(solution)/shard_map/reduce_scatter | solution.py:150
  276.1 2.9 fusion.6
  285.0 3.4 add_convert_fusion.2
  291.0 2.8 select_select_fusion
  293.7 3.8 collective-permute-start.9
  299.0 2.7 collective-permute-done.9
  302.7 4.1 %collective-permute-start.10 = (bf16[256,512]{0,1:T(8,128)(2,1)S(1)}, bf16[256,512]{0,1:T(8,128)(2,1)S(1)}, u32[]{:S(2)}, u32[]{:S(2)}) collective-permute-start(bf16[256,512]{0,1:T(8,128)(2,1)S(1)} %broadcast_select_fusion.7), channel_id=1, source_target_pairs={{8,0},{16,8},{24,16},{32,24},{40,32},{48,40},{56,48},{64,56},{72,6... | collective-permute-start | bytes 786440 | tf_op jit(solution)/shard_map/ppermute | solution.py:12
  310.7 4.2 %collective-permute-start.11 = (bf16[256,512]{0,1:T(8,128)(2,1)S(1)}, bf16[256,512]{0,1:T(8,128)(2,1)S(1)}, u32[]{:S(2)}, u32[]{:S(2)}) collective-permute-start(bf16[256,512]{0,1:T(8,128)(2,1)S(1)} %broadcast_select_fusion.6), channel_id=1, source_target_pairs={{8,0},{16,8},{24,16},{32,24},{40,32},{48,40},{56,48},{64,56},{72,6... | collective-permute-start | bytes 786440 | tf_op jit(solution)/shard_map/ppermute | solution.py:12
  322.2 3.8 %collective-permute-start.13 = (bf16[2,512]{0,1:T(8,128)(2,1)S(1)}, bf16[2,512]{0,1:T(8,128)(2,1)S(1)}, u32[]{:S(2)}, u32[]{:S(2)}) collective-permute-start(bf16[2,512]{0,1:T(8,128)(2,1)S(1)} %slice.292), channel_id=1, source_target_pairs={{8,0},{16,8},{24,16},{32,24},{40,32},{48,40},{56,48},{64,56},{72,6... | collective-permute-start | bytes 6152 | tf_op jit(solution)/shard_map/ppermute | solution.py:12
  329.5 3.8 collective-permute-start.12
  337.2 31.4 %all-gather.3.cloned.1.call-done = bf16[256,4096]{0,1:T(8,128)(2,1)} async-done(((bf16[256,512]{0,1:T(8,128)(2,1)}), bf16[256,4096]{0,1:T(8,128)(2,1)}) %all-gather.3.cloned.1.call-update) | async-done | bytes 2097168 | tf_op jit(solution)/shard_map/all_gather | solution.py:145
  368.6 4.8 %convolution_convert_fusion = bf16[256,512]{1,0:T(8,128)(2,1)} fusion(bf16[256,4096]{0,1:T(8,128)(2,1)} %all-gather.3.cloned.1.call-done, bf16[4096,512]{1,0:T(8,128)(2,1)} %all-gather.5.cloned.1.call-done), kind=kOutput, calls=%fused_computation | convolution fusion | flops 1073872896 | bytes 6553600 | tf_op jit(solution)/shard_map/dot_general | solution.py:144
  (132 shorter events, 71.6 us)
Async XLA Ops:
  7.2 126.5 %copy-start = (bf16[256,512]{1,0:T(8,128)(2,1)S(1)}, bf16[256,512]{1,0:T(8,128)(2,1)}, u32[]{:S(2)}) copy-start(bf16[256,512]{1,0:T(8,128)(2,1)} %param.17) | copy-start | bytes 786436
  7.2 126.4 %all-gather.5.cloned.1.call-start = ((), (), s32[]{:S(2)}) async-start(), calls=%async_computation.2 | async-start | bytes 4259840 | tf_op jit(solution)/shard_map/all_gather | solution.py:142
  7.9 268.2 %reduce-scatter.2.cloned.1.call-start = ((), (), s32[]{:S(2)}) async-start(), calls=%async_computation.3 | async-start | bytes 4718592 | tf_op jit(solution)/shard_map/reduce_scatter | solution.py:150
  139.2 229.4 %all-gather.3.cloned.1.call-start = ((), (), s32[]{:S(2)}) async-start(), calls=%async_computation.1 | async-start | bytes 2359296 | tf_op jit(solution)/shard_map/all_gather | solution.py:145
  140.4 20.1 %collective-permute-start.4 = (s32[2]{0:T(128)}, s32[2]{0:T(128)}, u32[]{:S(2)}, u32[]{:S(2)}) collective-permute-start(s32[2]{0:T(128)} %get-tuple-element.55), channel_id=1, source_target_pairs={{8,0},{16,8},{24,16},{32,24},{40,32},{48,40},{56,48},{64,56},{72,6... | collective-permute-start | bytes 32 | tf_op jit(solution)/shard_map/ppermute | solution.py:12
  144.0 17.1 %collective-permute-start = (s32[2]{0:T(128)}, s32[2]{0:T(128)}, u32[]{:S(2)}, u32[]{:S(2)}) collective-permute-start(s32[2]{0:T(128)} %get-tuple-element.54), channel_id=1, source_target_pairs={{0,8},{8,16},{16,24},{24,32},{32,40},{40,48},{48,56},{56,64},{64,7... | collective-permute-start | bytes 32 | tf_op jit(solution)/shard_map/ppermute | solution.py:12
  147.5 136.5 %collective-permute-start.1 = (bf16[2,512]{0,1:T(8,128)(2,1)}, bf16[2,512]{0,1:T(8,128)(2,1)}, u32[]{:S(2)}, u32[]{:S(2)}) collective-permute-start(bf16[2,512]{0,1:T(8,128)(2,1)} %copy.26), channel_id=1, source_target_pairs={{0,8},{8,16},{16,24},{24,32},{32,40},{40,48},{48,56},{56,64},{64,7... | collective-permute-start | bytes 6152 | tf_op jit(solution)/shard_map/ppermute | solution.py:12
  150.5 14.5 %collective-permute-start.2 = (bf16[2,512]{0,1:T(8,128)(2,1)}, bf16[2,512]{0,1:T(8,128)(2,1)}, u32[]{:S(2)}, u32[]{:S(2)}) collective-permute-start(bf16[2,512]{0,1:T(8,128)(2,1)} %copy.29), channel_id=1, source_target_pairs={{0,8},{8,16},{16,24},{24,32},{32,40},{40,48},{48,56},{56,64},{64,7... | collective-permute-start | bytes 6152 | tf_op jit(solution)/shard_map/ppermute | solution.py:12
  153.3 11.7 %collective-permute-start.3 = (bf16[2,512]{0,1:T(8,128)(2,1)}, bf16[2,512]{0,1:T(8,128)(2,1)S(1)}, u32[]{:S(2)}, u32[]{:S(2)}) collective-permute-start(bf16[2,512]{0,1:T(8,128)(2,1)} %copy.32), channel_id=1, source_target_pairs={{0,8},{8,16},{16,24},{24,32},{32,40},{40,48},{48,56},{56,64},{64,7... | collective-permute-start | bytes 6152 | tf_op jit(solution)/shard_map/ppermute | solution.py:12
  168.3 29.3 %collective-permute-start.5 = (bf16[256,512]{0,1:T(8,128)(2,1)}, bf16[256,512]{0,1:T(8,128)(2,1)}, u32[]{:S(2)}, u32[]{:S(2)}) collective-permute-start(bf16[256,512]{0,1:T(8,128)(2,1)} %get-tuple-element.18), channel_id=1, source_target_pairs={{0,8},{8,16},{16,24},{24,32},{32,40},{40,48},{48,56},{56,64},{64,7... | collective-permute-start | bytes 786440 | tf_op jit(solution)/shard_map/ppermute | solution.py:12
  198.6 7.9 %collective-permute-start.6 = (bf16[256,512]{0,1:T(8,128)(2,1)S(1)}, bf16[256,512]{0,1:T(8,128)(2,1)S(1)}, u32[]{:S(2)}, u32[]{:S(2)}) collective-permute-start(bf16[256,512]{0,1:T(8,128)(2,1)S(1)} %broadcast_select_fusion.9), channel_id=1, source_target_pairs={{0,8},{8,16},{16,24},{24,32},{32,40},{40,48},{48,56},{56,64},{64,7... | collective-permute-start | bytes 786440 | tf_op jit(solution)/shard_map/ppermute | solution.py:12
  206.5 78.6 %copy-start.10 = (pred[256]{0:T(512)(128)(4,1)S(1)}, pred[256]{0:T(512)(128)(4,1)}, u32[]{:S(2)}) copy-start(pred[256]{0:T(512)(128)(4,1)} %get-tuple-element.45) | copy-start | bytes 772
  206.5 7.7 %collective-permute-start.7 = (bf16[256,512]{0,1:T(8,128)(2,1)S(1)}, bf16[256,512]{0,1:T(8,128)(2,1)S(1)}, u32[]{:S(2)}, u32[]{:S(2)}) collective-permute-start(bf16[256,512]{0,1:T(8,128)(2,1)S(1)} %broadcast_select_fusion.8), channel_id=1, source_target_pairs={{0,8},{8,16},{16,24},{24,32},{32,40},{40,48},{48,56},{56,64},{64,7... | collective-permute-start | bytes 786440 | tf_op jit(solution)/shard_map/ppermute | solution.py:12
  280.3 4.7 %collective-permute-start.8 = (bf16[2,512]{0,1:T(8,128)(2,1)}, bf16[2,512]{0,1:T(8,128)(2,1)}, u32[]{:S(2)}, u32[]{:S(2)}) collective-permute-start(bf16[2,512]{0,1:T(8,128)(2,1)} %slice.286), channel_id=1, source_target_pairs={{8,0},{16,8},{24,16},{32,24},{40,32},{48,40},{56,48},{64,56},{72,6... | collective-permute-start | bytes 6152 | tf_op jit(solution)/shard_map/ppermute | solution.py:12
  293.7 8.0 %collective-permute-start.9 = (bf16[256,512]{0,1:T(8,128)(2,1)}, bf16[256,512]{0,1:T(8,128)(2,1)}, u32[]{:S(2)}, u32[]{:S(2)}) collective-permute-start(bf16[256,512]{0,1:T(8,128)(2,1)} %get-tuple-element.14), channel_id=1, source_target_pairs={{8,0},{16,8},{24,16},{32,24},{40,32},{48,40},{56,48},{64,56},{72,6... | collective-permute-start | bytes 786440 | tf_op jit(solution)/shard_map/ppermute | solution.py:12
  297.5 22.9 %copy-start.2 = (bf16[256,512]{0,1:T(8,128)(2,1)S(1)}, bf16[256,512]{0,1:T(8,128)(2,1)}, u32[]{:S(2)}) copy-start(bf16[256,512]{0,1:T(8,128)(2,1)} %copy.28) | copy-start | bytes 786436
  297.5 22.9 %copy-start.5 = (bf16[256,512]{0,1:T(8,128)(2,1)S(1)}, bf16[256,512]{0,1:T(8,128)(2,1)}, u32[]{:S(2)}) copy-start(bf16[256,512]{0,1:T(8,128)(2,1)} %get-tuple-element.15) | copy-start | bytes 786436
  302.7 8.0 %collective-permute-start.10 = (bf16[256,512]{0,1:T(8,128)(2,1)S(1)}, bf16[256,512]{0,1:T(8,128)(2,1)S(1)}, u32[]{:S(2)}, u32[]{:S(2)}) collective-permute-start(bf16[256,512]{0,1:T(8,128)(2,1)S(1)} %broadcast_select_fusion.7), channel_id=1, source_target_pairs={{8,0},{16,8},{24,16},{32,24},{40,32},{48,40},{56,48},{64,56},{72,6... | collective-permute-start | bytes 786440 | tf_op jit(solution)/shard_map/ppermute | solution.py:12
  308.4 20.1 %copy-start.14 = (f32[1,1,512]{2,1,0:T(1,128)S(1)}, f32[1,1,512]{2,1,0:T(1,128)}, u32[]{:S(2)}) copy-start(f32[1,1,512]{2,1,0:T(1,128)} %get-tuple-element.28) | copy-start | bytes 6148
  308.5 20.1 %copy-start.16 = (pred[256]{0:T(512)(128)(4,1)S(1)}, pred[256]{0:T(512)(128)(4,1)}, u32[]{:S(2)}) copy-start(pred[256]{0:T(512)(128)(4,1)} %get-tuple-element.39) | copy-start | bytes 772
  308.5 20.1 %copy-start.18 = (pred[256]{0:T(512)(128)(4,1)S(1)}, pred[256]{0:T(512)(128)(4,1)}, u32[]{:S(2)}) copy-start(pred[256]{0:T(512)(128)(4,1)} %get-tuple-element.40) | copy-start | bytes 772
  310.7 8.1 %collective-permute-start.11 = (bf16[256,512]{0,1:T(8,128)(2,1)S(1)}, bf16[256,512]{0,1:T(8,128)(2,1)S(1)}, u32[]{:S(2)}, u32[]{:S(2)}) collective-permute-start(bf16[256,512]{0,1:T(8,128)(2,1)S(1)} %broadcast_select_fusion.6), channel_id=1, source_target_pairs={{8,0},{16,8},{24,16},{32,24},{40,32},{48,40},{56,48},{64,56},{72,6... | collective-permute-start | bytes 786440 | tf_op jit(solution)/shard_map/ppermute | solution.py:12
  322.2 6.3 %collective-permute-start.13 = (bf16[2,512]{0,1:T(8,128)(2,1)S(1)}, bf16[2,512]{0,1:T(8,128)(2,1)S(1)}, u32[]{:S(2)}, u32[]{:S(2)}) collective-permute-start(bf16[2,512]{0,1:T(8,128)(2,1)S(1)} %slice.292), channel_id=1, source_target_pairs={{8,0},{16,8},{24,16},{32,24},{40,32},{48,40},{56,48},{64,56},{72,6... | collective-permute-start | bytes 6152 | tf_op jit(solution)/shard_map/ppermute | solution.py:12
  329.5 6.3 %collective-permute-start.12 = (bf16[2,512]{0,1:T(8,128)(2,1)S(1)}, bf16[2,512]{0,1:T(8,128)(2,1)S(1)}, u32[]{:S(2)}, u32[]{:S(2)}) collective-permute-start(bf16[2,512]{0,1:T(8,128)(2,1)S(1)} %slice.289), channel_id=1, source_target_pairs={{8,0},{16,8},{24,16},{32,24},{40,32},{48,40},{56,48},{64,56},{72,6... | collective-permute-start | bytes 6152 | tf_op jit(solution)/shard_map/ppermute | solution.py:12
  (15 other events, 199.5 us)
Sparse Core Ops, SparseCore 0:
  10.1 123.4 all-gather.4
  139.3 136.7 reduce-scatter.1
  288.6 79.9 all-gather.2
where the time goes:
time: 381 us; the launch traced here: 380 us
  waiting for transfers between devices  230 us (60%)
  starting transfers between devices  41.9 us (11%)
  local copies, waits for them, and re-layouts  38.2 us (10%)
  other arithmetic  28.2 us (7%)
  matrix products  23.8 us (6%)
  between operations  17.9 us (5%)
    all_gather x1, waiting for transfers between devices, local(): weight_rows = lax.all_gather(out_weight, 'ctx', axis=0, tiled=True)  126 us
    reduce_scatter x1, waiting for transfers between devices, local(): lax.psum_scatter(lax.dot_general(matched, out_grad, (((1,), (1,)), ((), (...  59.5 us
    ppermute x14, starting transfers between devices, shifted(): return lax.ppermute(array, axis, pairs)  41.8 us
    all_gather x1, waiting for transfers between devices, local(): lax.all_gather(pre_gate, 'ch', axis=1, tiled=True)  31.4 us
    reshape x4, local copies, waits for them, and re-layouts, toeplitz_tiles(): repeated.reshape(group_count, row_count, 2 * row_count - 1)  13.2 us
    unnamed x58, local copies, waits for them, and re-layouts  13.2 us
    ppermute x14, waiting for transfers between devices, shifted(): return lax.ppermute(array, axis, pairs)  12.5 us
    dot_general x4, matrix products, apply_forward(): jnp.einsum('gst,sgc->tgc', band_tile, grouped, preferred_element_type=jnp...  8.18 us
  transfers between devices with their start and end apart: 17, of which 10 were waited for; matrix products, arithmetic and copies ran while one was open for 20% of the time, Pallas kernels for 0%

commit v1 on v0

--- a/solution.py
+++ b/solution.py
@@ -4,6 +4,13 @@
 from jax.sharding import PartitionSpec as P
 
 HOPS = 3
+
+
+def pass_the_scenes(raw):
+    return jnp.concatenate(
+        lax.all_to_all(jnp.stack(tuple((raw for _ in range(lax.axis_size("ch"))))), "ch", 0, 0),
+        axis=1,
+    )
 
 
 def shifted(array, axis, by):
@@ -141,11 +148,7 @@
     pre_gate = (query_short * mixed).astype(jnp.bfloat16)
     weight_rows = lax.all_gather(out_weight, "ctx", axis=0, tiled=True)
     matched = weight_rows
-    out_sum = jnp.dot(
-        lax.all_gather(pre_gate, "ch", axis=1, tiled=True),
-        matched,
-        preferred_element_type=jnp.float32,
-    )
+    out_sum = jnp.dot(pass_the_scenes(pre_gate), matched, preferred_element_type=jnp.float32)
     matched = weight_rows
     grad_cols = lax.psum_scatter(
         lax.dot_general(

time: 381 us -> 370 us (0.971)
  the two profiles are of different devices: /device:TPU:8 before, /device:TPU:121 now
where the time goes in v1:
time: 370 us; the launch traced here: 368 us
  waiting for transfers between devices  215 us (58%)
  starting transfers between devices  44.5 us (12%)
  local copies, waits for them, and re-layouts  39.9 us (11%)
  other arithmetic  26.5 us (7%)
  matrix products  23.8 us (6%)
  between operations  18.3 us (5%)
    all_gather x1, waiting for transfers between devices, local(): weight_rows = lax.all_gather(out_weight, 'ctx', axis=0, tiled=True)  124 us
    reduce_scatter x1, waiting for transfers between devices, local(): lax.psum_scatter(lax.dot_general(matched, out_grad, (((1,), (1,)), ((), (...  54.4 us
    ppermute x14, starting transfers between devices, shifted(): return lax.ppermute(array, axis, pairs)  40 us
    ppermute x14, waiting for transfers between devices, shifted(): return lax.ppermute(array, axis, pairs)  35.8 us
    reshape x4, local copies, waits for them, and re-layouts, toeplitz_tiles(): repeated.reshape(group_count, row_count, 2 * row_count - 1)  13.2 us
    unnamed x58, local copies, waits for them, and re-layouts  13.2 us
    dot_general x4, matrix products, apply_forward(): jnp.einsum('gst,sgc->tgc', band_tile, grouped, preferred_element_type=jnp...  8.21 us
  transfers between devices with their start and end apart: 17, of which 10 were waited for; matrix products, arithmetic and copies ran while one was open for 20% of the time, Pallas kernels for 0%

profile of v1, /device:TPU:121, one launch (start us, length us, event | category | flops | bytes accessed | tf_op | source)
XLA Modules:
  0.0 368.2 jit_solution(11702797434304522599)
XLA Ops:
  8.0 123.5 %all-gather.2.cloned.1.call-done = bf16[4096,512]{1,0:T(8,128)(2,1)} async-done(((bf16[64,512]{1,0:T(8,128)(2,1)}), bf16[4096,512]{1,0:T(8,128)(2,1)}) %all-gather.2.cloned.1.call-update) | async-done | bytes 4194320 | tf_op jit(solution)/shard_map/all_gather | solution.py:149
  131.5 5.5 %fusion.39 = f32[4096,256]{1,0:T(8,128)} fusion(bf16[4096,512]{1,0:T(8,128)(2,1)} %all-gather.2.cloned.1.call-done, bf16[256,512]{1,0:T(8,128)(2,1)S(1)} %copy-done), kind=kOutput, calls=%fused_computation.116 | convolution fusion | flops 1073741824 | bytes 8650752 | tf_op jit(solution)/shard_map/dot_general | solution.py:154
  140.5 5.5 %collective-permute-start = (s32[2]{0:T(128)}, s32[2]{0:T(128)}, u32[]{:S(2)}, u32[]{:S(2)}) collective-permute-start(s32[2]{0:T(128)} %get-tuple-element.54), channel_id=1, source_target_pairs={{0,8},{8,16},{16,24},{24,32},{32,40},{40,48},{48,56},{56,64},{64,7... | collective-permute-start | bytes 32 | tf_op jit(solution)/shard_map/ppermute | solution.py:19
  150.2 2.7 collective-permute-start.2
  164.9 3.3 select_select_fusion.1
  168.2 2.7 collective-permute-start.5
  175.1 3.1 reshape.158
  180.4 3.0 reshape.156
  185.6 3.1 reshape.154
  192.0 4.0 %reshape.151 = bf16[4,256,511]{2,1,0:T(8,128)(2,1)} reshape(bf16[4,130816]{1,0:T(4,128)(2,1)} %slice.278) | data formatting | bytes 2093056 | tf_op jit(solution)/shard_map/reshape | solution.py:45
  204.5 7.7 %collective-permute-start.7 = (bf16[256,512]{0,1:T(8,128)(2,1)S(1)}, bf16[256,512]{0,1:T(8,128)(2,1)S(1)}, u32[]{:S(2)}, u32[]{:S(2)}) collective-permute-start(bf16[256,512]{0,1:T(8,128)(2,1)S(1)} %broadcast_select_fusion.8), channel_id=1, source_target_pairs={{0,8},{8,16},{16,24},{24,32},{32,40},{40,48},{48,56},{56,64},{64,7... | collective-permute-start | bytes 786440 | tf_op jit(solution)/shard_map/ppermute | solution.py:19
  218.0 54.4 %reduce-scatter.2.cloned.1.call-done = f32[512,256]{1,0:T(8,128)} async-done(((f32[4096,256]{1,0:T(8,128)}), f32[512,256]{1,0:T(8,128)}) %reduce-scatter.2.cloned.1.call-update) | async-done | bytes 524304 | tf_op jit(solution)/shard_map/reduce_scatter | solution.py:153
  272.5 2.8 fusion.6
  276.6 3.9 %collective-permute-start.8 = (bf16[2,512]{0,1:T(8,128)(2,1)}, bf16[2,512]{0,1:T(8,128)(2,1)}, u32[]{:S(2)}, u32[]{:S(2)}) collective-permute-start(bf16[2,512]{0,1:T(8,128)(2,1)} %slice.286), channel_id=1, source_target_pairs={{8,0},{16,8},{24,16},{32,24},{40,32},{48,40},{56,48},{64,56},{72,6... | collective-permute-start | bytes 6152 | tf_op jit(solution)/shard_map/ppermute | solution.py:19
  282.4 3.0 collective-permute-done.8
  285.3 3.5 add_convert_fusion.2
  290.3 4.4 %all-to-all-start = ((bf16[8,256,512]{1,2,0:T(8,128)(2,1)}), bf16[8,256,512]{1,2,0:T(8,128)(2,1)}, u32[]{:S(2)}, u32[]{:S(2)}) async-start(bf16[8,256,512]{1,2,0:T(8,128)(2,1)} %stack.2), calls=%async_computation | async-start | bytes 4194304 | tf_op jit(solution)/shard_map/all_to_all | solution.py:11
  297.2 2.8 select_select_fusion
  303.5 7.2 %collective-permute-done.9 = bf16[256,512]{0,1:T(8,128)(2,1)} collective-permute-done((bf16[256,512]{0,1:T(8,128)(2,1)}, bf16[256,512]{0,1:T(8,128)(2,1)}, u32[]{:S(2)}, u32[]{:S(2)}) %collective-permute-start.9) | collective-permute-done | bytes 262176 | tf_op jit(solution)/shard_map/ppermute | solution.py:19
  316.2 4.7 %collective-permute-done.10 = bf16[256,512]{0,1:T(8,128)(2,1)S(1)} collective-permute-done((bf16[256,512]{0,1:T(8,128)(2,1)S(1)}, bf16[256,512]{0,1:T(8,128)(2,1)S(1)}, u32[]{:S(2)}, u32[]{:S(2)}) %collective-permute-start.10) | collective-permute-done | bytes 262176 | tf_op jit(solution)/shard_map/ppermute | solution.py:19
  324.6 6.7 %collective-permute-done.11 = bf16[256,512]{0,1:T(8,128)(2,1)S(1)} collective-permute-done((bf16[256,512]{0,1:T(8,128)(2,1)S(1)}, bf16[256,512]{0,1:T(8,128)(2,1)S(1)}, u32[]{:S(2)}, u32[]{:S(2)}) %collective-permute-start.11) | collective-permute-done | bytes 262176 | tf_op jit(solution)/shard_map/ppermute | solution.py:19
  336.7 7.4 %collective-permute-done.13 = bf16[2,512]{0,1:T(8,128)(2,1)S(1)} collective-permute-done((bf16[2,512]{0,1:T(8,128)(2,1)S(1)}, bf16[2,512]{0,1:T(8,128)(2,1)S(1)}, u32[]{:S(2)}, u32[]{:S(2)}) %collective-permute-start.13) | collective-permute-done | bytes 2080 | tf_op jit(solution)/shard_map/ppermute | solution.py:19
  348.7 5.8 %collective-permute-done.12 = bf16[2,512]{0,1:T(8,128)(2,1)S(1)} collective-permute-done((bf16[2,512]{0,1:T(8,128)(2,1)S(1)}, bf16[2,512]{0,1:T(8,128)(2,1)S(1)}, u32[]{:S(2)}, u32[]{:S(2)}) %collective-permute-start.12) | collective-permute-done | bytes 2080 | tf_op jit(solution)/shard_map/ppermute | solution.py:19
  356.6 4.8 %convolution_convert_fusion = bf16[256,512]{1,0:T(8,128)(2,1)} fusion(bf16[256,4096]{0,1:T(8,128)(2,1)} %bitcast.25, bf16[4096,512]{1,0:T(8,128)(2,1)} %all-gather.2.cloned.1.call-done), kind=kOutput, calls=%fused_computation | convolution fusion | flops 1073872896 | bytes 6553600 | tf_op jit(solution)/shard_map/dot_general | solution.py:151
  (132 shorter events, 74.4 us)
Async XLA Ops:
  7.2 124.3 %copy-start = (bf16[256,512]{1,0:T(8,128)(2,1)S(1)}, bf16[256,512]{1,0:T(8,128)(2,1)}, u32[]{:S(2)}) copy-start(bf16[256,512]{1,0:T(8,128)(2,1)} %param.17) | copy-start | bytes 786436
  7.2 124.3 %all-gather.2.cloned.1.call-start = ((), (), s32[]{:S(2)}) async-start(), calls=%async_computation.2 | async-start | bytes 4259840 | tf_op jit(solution)/shard_map/all_gather | solution.py:149
  7.9 264.6 %reduce-scatter.2.cloned.1.call-start = ((), (), s32[]{:S(2)}) async-start(), calls=%async_computation.3 | async-start | bytes 4718592 | tf_op jit(solution)/shard_map/reduce_scatter | solution.py:153
  138.3 22.0 %collective-permute-start.4 = (s32[2]{0:T(128)}, s32[2]{0:T(128)}, u32[]{:S(2)}, u32[]{:S(2)}) collective-permute-start(s32[2]{0:T(128)} %get-tuple-element.55), channel_id=1, source_target_pairs={{8,0},{16,8},{24,16},{32,24},{40,32},{48,40},{56,48},{64,56},{72,6... | collective-permute-start | bytes 32 | tf_op jit(solution)/shard_map/ppermute | solution.py:19
  140.5 20.5 %collective-permute-start = (s32[2]{0:T(128)}, s32[2]{0:T(128)}, u32[]{:S(2)}, u32[]{:S(2)}) collective-permute-start(s32[2]{0:T(128)} %get-tuple-element.54), channel_id=1, source_target_pairs={{0,8},{8,16},{16,24},{24,32},{32,40},{40,48},{48,56},{56,64},{64,7... | collective-permute-start | bytes 32 | tf_op jit(solution)/shard_map/ppermute | solution.py:19
  147.5 134.9 %collective-permute-start.1 = (bf16[2,512]{0,1:T(8,128)(2,1)}, bf16[2,512]{0,1:T(8,128)(2,1)}, u32[]{:S(2)}, u32[]{:S(2)}) collective-permute-start(bf16[2,512]{0,1:T(8,128)(2,1)} %copy.27), channel_id=1, source_target_pairs={{0,8},{8,16},{16,24},{24,32},{32,40},{40,48},{48,56},{56,64},{64,7... | collective-permute-start | bytes 6152 | tf_op jit(solution)/shard_map/ppermute | solution.py:19
  150.2 14.6 %collective-permute-start.2 = (bf16[2,512]{0,1:T(8,128)(2,1)}, bf16[2,512]{0,1:T(8,128)(2,1)}, u32[]{:S(2)}, u32[]{:S(2)}) collective-permute-start(bf16[2,512]{0,1:T(8,128)(2,1)} %copy.30), channel_id=1, source_target_pairs={{0,8},{8,16},{16,24},{24,32},{32,40},{40,48},{48,56},{56,64},{64,7... | collective-permute-start | bytes 6152 | tf_op jit(solution)/shard_map/ppermute | solution.py:19
  153.8 11.1 %collective-permute-start.3 = (bf16[2,512]{0,1:T(8,128)(2,1)}, bf16[2,512]{0,1:T(8,128)(2,1)S(1)}, u32[]{:S(2)}, u32[]{:S(2)}) collective-permute-start(bf16[2,512]{0,1:T(8,128)(2,1)} %copy.33), channel_id=1, source_target_pairs={{0,8},{8,16},{16,24},{24,32},{32,40},{40,48},{48,56},{56,64},{64,7... | collective-permute-start | bytes 6152 | tf_op jit(solution)/shard_map/ppermute | solution.py:19
  168.2 30.0 %collective-permute-start.5 = (bf16[256,512]{0,1:T(8,128)(2,1)}, bf16[256,512]{0,1:T(8,128)(2,1)}, u32[]{:S(2)}, u32[]{:S(2)}) collective-permute-start(bf16[256,512]{0,1:T(8,128)(2,1)} %get-tuple-element.18), channel_id=1, source_target_pairs={{0,8},{8,16},{16,24},{24,32},{32,40},{40,48},{48,56},{56,64},{64,7... | collective-permute-start | bytes 786440 | tf_op jit(solution)/shard_map/ppermute | solution.py:19
  198.3 6.2 %collective-permute-start.6 = (bf16[256,512]{0,1:T(8,128)(2,1)S(1)}, bf16[256,512]{0,1:T(8,128)(2,1)S(1)}, u32[]{:S(2)}, u32[]{:S(2)}) collective-permute-start(bf16[256,512]{0,1:T(8,128)(2,1)S(1)} %broadcast_select_fusion.9), channel_id=1, source_target_pairs={{0,8},{8,16},{16,24},{24,32},{32,40},{40,48},{48,56},{56,64},{64,7... | collective-permute-start | bytes 786440 | tf_op jit(solution)/shard_map/ppermute | solution.py:19
  204.5 80.9 %copy-start.10 = (pred[256]{0:T(512)(128)(4,1)S(1)}, pred[256]{0:T(512)(128)(4,1)}, u32[]{:S(2)}) copy-start(pred[256]{0:T(512)(128)(4,1)} %get-tuple-element.45) | copy-start | bytes 772
  204.5 11.1 %collective-permute-start.7 = (bf16[256,512]{0,1:T(8,128)(2,1)S(1)}, bf16[256,512]{0,1:T(8,128)(2,1)S(1)}, u32[]{:S(2)}, u32[]{:S(2)}) collective-permute-start(bf16[256,512]{0,1:T(8,128)(2,1)S(1)} %broadcast_select_fusion.8), channel_id=1, source_target_pairs={{0,8},{8,16},{16,24},{24,32},{32,40},{40,48},{48,56},{56,64},{64,7... | collective-permute-start | bytes 786440 | tf_op jit(solution)/shard_map/ppermute | solution.py:19
  276.6 8.7 %collective-permute-start.8 = (bf16[2,512]{0,1:T(8,128)(2,1)}, bf16[2,512]{0,1:T(8,128)(2,1)}, u32[]{:S(2)}, u32[]{:S(2)}) collective-permute-start(bf16[2,512]{0,1:T(8,128)(2,1)} %slice.286), channel_id=1, source_target_pairs={{8,0},{16,8},{24,16},{32,24},{40,32},{48,40},{56,48},{64,56},{72,6... | collective-permute-start | bytes 6152 | tf_op jit(solution)/shard_map/ppermute | solution.py:19
  290.3 66.3 %all-to-all-start = ((bf16[8,256,512]{1,2,0:T(8,128)(2,1)}), bf16[8,256,512]{1,2,0:T(8,128)(2,1)}, u32[]{:S(2)}, u32[]{:S(2)}) async-start(bf16[8,256,512]{1,2,0:T(8,128)(2,1)} %stack.2), calls=%async_computation | async-start | bytes 4194304 | tf_op jit(solution)/shard_map/all_to_all | solution.py:11
  300.0 10.6 %collective-permute-start.9 = (bf16[256,512]{0,1:T(8,128)(2,1)}, bf16[256,512]{0,1:T(8,128)(2,1)}, u32[]{:S(2)}, u32[]{:S(2)}) collective-permute-start(bf16[256,512]{0,1:T(8,128)(2,1)} %get-tuple-element.14), channel_id=1, source_target_pairs={{8,0},{16,8},{24,16},{32,24},{40,32},{48,40},{56,48},{64,56},{72,6... | collective-permute-start | bytes 786440 | tf_op jit(solution)/shard_map/ppermute | solution.py:19
  302.0 31.0 %copy-start.2 = (bf16[256,512]{0,1:T(8,128)(2,1)S(1)}, bf16[256,512]{0,1:T(8,128)(2,1)}, u32[]{:S(2)}) copy-start(bf16[256,512]{0,1:T(8,128)(2,1)} %copy.29) | copy-start | bytes 786436
  302.0 31.0 %copy-start.5 = (bf16[256,512]{0,1:T(8,128)(2,1)S(1)}, bf16[256,512]{0,1:T(8,128)(2,1)}, u32[]{:S(2)}) copy-start(bf16[256,512]{0,1:T(8,128)(2,1)} %get-tuple-element.15) | copy-start | bytes 786436
  310.7 10.3 %collective-permute-start.10 = (bf16[256,512]{0,1:T(8,128)(2,1)S(1)}, bf16[256,512]{0,1:T(8,128)(2,1)S(1)}, u32[]{:S(2)}, u32[]{:S(2)}) collective-permute-start(bf16[256,512]{0,1:T(8,128)(2,1)S(1)} %broadcast_select_fusion.7), channel_id=1, source_target_pairs={{8,0},{16,8},{24,16},{32,24},{40,32},{48,40},{56,48},{64,56},{72,6... | collective-permute-start | bytes 786440 | tf_op jit(solution)/shard_map/ppermute | solution.py:19
  314.3 29.9 %copy-start.14 = (f32[1,1,512]{2,1,0:T(1,128)S(1)}, f32[1,1,512]{2,1,0:T(1,128)}, u32[]{:S(2)}) copy-start(f32[1,1,512]{2,1,0:T(1,128)} %get-tuple-element.28) | copy-start | bytes 6148
  314.3 29.9 %copy-start.16 = (pred[256]{0:T(512)(128)(4,1)S(1)}, pred[256]{0:T(512)(128)(4,1)}, u32[]{:S(2)}) copy-start(pred[256]{0:T(512)(128)(4,1)} %get-tuple-element.39) | copy-start | bytes 772
  314.3 29.9 %copy-start.18 = (pred[256]{0:T(512)(128)(4,1)S(1)}, pred[256]{0:T(512)(128)(4,1)}, u32[]{:S(2)}) copy-start(pred[256]{0:T(512)(128)(4,1)} %get-tuple-element.40) | copy-start | bytes 772
  321.0 10.3 %collective-permute-start.11 = (bf16[256,512]{0,1:T(8,128)(2,1)S(1)}, bf16[256,512]{0,1:T(8,128)(2,1)S(1)}, u32[]{:S(2)}, u32[]{:S(2)}) collective-permute-start(bf16[256,512]{0,1:T(8,128)(2,1)S(1)} %broadcast_select_fusion.6), channel_id=1, source_target_pairs={{8,0},{16,8},{24,16},{32,24},{40,32},{48,40},{56,48},{64,56},{72,6... | collective-permute-start | bytes 786440 | tf_op jit(solution)/shard_map/ppermute | solution.py:19
  334.8 9.3 %collective-permute-start.13 = (bf16[2,512]{0,1:T(8,128)(2,1)S(1)}, bf16[2,512]{0,1:T(8,128)(2,1)S(1)}, u32[]{:S(2)}, u32[]{:S(2)}) collective-permute-start(bf16[2,512]{0,1:T(8,128)(2,1)S(1)} %slice.292), channel_id=1, source_target_pairs={{8,0},{16,8},{24,16},{32,24},{40,32},{48,40},{56,48},{64,56},{72,6... | collective-permute-start | bytes 6152 | tf_op jit(solution)/shard_map/ppermute | solution.py:19
  345.0 9.4 %collective-permute-start.12 = (bf16[2,512]{0,1:T(8,128)(2,1)S(1)}, bf16[2,512]{0,1:T(8,128)(2,1)S(1)}, u32[]{:S(2)}, u32[]{:S(2)}) collective-permute-start(bf16[2,512]{0,1:T(8,128)(2,1)S(1)} %slice.289), channel_id=1, source_target_pairs={{8,0},{16,8},{24,16},{32,24},{40,32},{48,40},{56,48},{64,56},{72,6... | collective-permute-start | bytes 6152 | tf_op jit(solution)/shard_map/ppermute | solution.py:19
  (15 other events, 264.6 us)
Sparse Core Ops, SparseCore 0:
  10.1 121.3 all-gather.1
  137.2 135.2 reduce-scatter.1
